TPU v7x, 256 devices: a whole 4x4x8 slice. The times are simulated.
256 devices in a mesh: src: 8 (over z_hi, y), width: 32 (over z_lo, x, core).
Axes of the slice: x: 4, y: 4, z: 8 (z_hi: 2, z_lo: 4; z = z_hi * 4 + z_lo), core: 2. Of those that a mesh axis runs over, the one named last changes fastest.
Arguments:
- resid: bfloat16 [8, 512, 8192], P('src', None, 'width'), may hold values from -6 to 6
- enc_w: bfloat16 [8, 8192, 6144], P('src', 'width'), may hold values from -0.0625 to 0.0625
- enc_b: float32 [8, 6144], P('src'), may hold values from -3 to 3
- dec_w: bfloat16 [8, 6144, 8192], P('src', None, 'width'), may hold values from -0.078125 to 0.078125
- target: bfloat16 [512, 8192], P(None, 'width'), may hold values from -36 to 36
- norm_gain: float32 [8192], P('width'), may hold values from 0.5 to 1.5
- wq: bfloat16 [8192, 8192], P(None, 'width'), may hold values from -0.0625 to 0.0625
- wk: bfloat16 [8192, 1024], P('width'), may hold values from -0.0625 to 0.0625
- wv: bfloat16 [8192, 1024], P('width'), may hold values from -0.0625 to 0.0625
- prompt_ids: int32 [512], replicated, may hold values from 0 to 3, never falling along the last dimension, each value on 1 to 256 neighbouring positions
Outputs:
- mlp_out: bfloat16 [512, 8192], P('src', 'width')
- context: bfloat16 [512, 8192], P('src', 'width')
Inputs may be any that keep to these rules, and one draw needn't show every extreme that they name: `prompt_ids`: rows of one prompt are contiguous and numbered in increasing order; the longest prompt has 256 rows.
All inputs are finite; a program needn't handle non-finite values.
Results may differ from a plain program's by a relative error of at most 0.008.
Values may be sent and summed in bfloat16 or wider, within the bound.
No kernel may reach another device: no remote copies, remote signals or barrier semaphores. Data moves between devices by JAX's collectives and lax.ppermute only.
A program may use at most 128 MiB of HBM per device.

v0:
```python
import math
import jax
import jax.numpy as jnp
from jax import lax
from jax.sharding import Mesh
from jax.sharding import PartitionSpec as P

HD = 128
GROUP = 8
WIDTH = ("wc", "core")
SWAP = [(0, 1), (1, 0)]


def contract0(a, b):
    return lax.dot_general(a, b, (((0,), (0,)), ((), ())), preferred_element_type=jnp.float32)


def on_device(resid, enc_w, enc_b, dec_w, target, norm_gain, wq, wk, wv, prompt_ids):
    n_wc = lax.axis_size("wc")
    n_core = lax.axis_size("core")
    n_src = lax.axis_size("src")
    core = lax.axis_index("core")
    chip = lax.axis_index("wc")
    src = lax.axis_index("src")
    width_pos = chip * n_core + core
    rows_all = resid.shape[1]
    width_local = resid.shape[2]
    width_all = width_local * n_wc * n_core
    feats_all = enc_w.shape[2]
    half = feats_all // 2
    share = half // n_wc
    other = 1 - core
    x = resid[0]
    we = enc_w[0]
    we_mine = lax.dynamic_slice_in_dim(we, core * half, half, 1)
    we_give = lax.dynamic_slice_in_dim(we, other * half, half, 1)
    we_got = lax.ppermute(we_give, "core", SWAP)
    x_got = lax.ppermute(x, "core", SWAP)
    pre = lax.dot_general(we_mine, x, (((0,), (1,)), ((), ())), preferred_element_type=jnp.float32)
    pre = pre + lax.dot_general(
        we_got, x_got, (((0,), (1,)), ((), ())), preferred_element_type=jnp.float32
    )
    pre_share = lax.psum_scatter(pre, "wc", scatter_dimension=0, tiled=True)
    bias = lax.dynamic_slice_in_dim(enc_b[0], core * half + chip * share, share, 0)
    feats_t = jnp.maximum(pre_share + bias[:, None], 0.0).astype(jnp.bfloat16)
    feats_half = lax.all_gather(feats_t, "wc", axis=0, tiled=True)
    wd = dec_w[0]
    wd_mine = lax.dynamic_slice_in_dim(wd, core * half, half, 0)
    wd_give = lax.dynamic_slice_in_dim(wd, other * half, half, 0)
    wd_got = lax.ppermute(wd_give, "core", SWAP)
    part_mine = contract0(feats_half, wd_mine)
    part_other = contract0(feats_half, wd_got)
    mlp_layer = part_mine + lax.ppermute(part_other, "core", SWAP)
    query_rows = rows_all // n_src
    row_start = src * query_rows
    mlp = lax.psum_scatter(mlp_layer, "src", scatter_dimension=0, tiled=True)
    mlp_out = mlp.astype(jnp.bfloat16)
    tgt = lax.dynamic_slice_in_dim(target, row_start, query_rows, 0)
    stream = tgt.astype(jnp.float32) + mlp
    stream_full = lax.all_gather(stream, WIDTH, axis=1, tiled=True)
    gain_full = lax.all_gather(norm_gain, WIDTH, axis=0, tiled=True)
    power = jnp.sum(stream_full * stream_full, axis=1) / width_all
    scale = lax.rsqrt(power + 1e-05)[:, None]
    normed_full = (stream_full * scale * gain_full[None, :]).astype(jnp.bfloat16)
    normed_loc = (stream * scale * norm_gain[None, :]).astype(jnp.bfloat16)
    query = jnp.dot(normed_full, wq, preferred_element_type=jnp.float32).astype(jnp.bfloat16)
    key_part = jnp.dot(normed_loc, wk, preferred_element_type=jnp.float32)
    value_part = jnp.dot(normed_loc, wv, preferred_element_type=jnp.float32)
    key_total, value_total = lax.psum((key_part, value_part), WIDTH)
    heads_here = wq.shape[1] // HD
    kv_index = width_pos * heads_here // GROUP
    key_head = lax.dynamic_slice_in_dim(key_total, kv_index * HD, HD, 1).astype(jnp.bfloat16)
    value_head = lax.dynamic_slice_in_dim(value_total, kv_index * HD, HD, 1).astype(jnp.bfloat16)
    key_head = lax.all_gather(key_head, "src", axis=0, tiled=True)
    value_head = lax.all_gather(value_head, "src", axis=0, tiled=True)
    query3 = query.reshape(query_rows, heads_here, HD)
    scores = jnp.einsum(
        "qhd,sd->hqs", query3, key_head, preferred_element_type=jnp.float32
    ) / math.sqrt(HD)
    query_index = row_start + jnp.arange(query_rows, dtype=jnp.int32)
    key_index = jnp.arange(rows_all, dtype=jnp.int32)
    query_prompt = lax.dynamic_slice_in_dim(prompt_ids, row_start, query_rows, 0)
    allowed = (query_prompt[:, None] == prompt_ids[None, :]) & (
        key_index[None, :] <= query_index[:, None]
    )
    scores = jnp.where(allowed[None], scores, -1e30)
    peak = jnp.max(scores, axis=-1, keepdims=True)
    weights = jnp.exp(scores - peak)
    probs = (weights / jnp.sum(weights, axis=-1, keepdims=True)).astype(jnp.bfloat16)
    context = jnp.einsum("hqs,sd->qhd", probs, value_head, preferred_element_type=jnp.float32)
    return (mlp_out, context.reshape(query_rows, heads_here * HD).astype(jnp.bfloat16))


def solution(mesh):
    n_src = mesh.shape["src"]
    n_width = mesh.shape["width"]
    fine = Mesh(mesh.devices.reshape(n_src, n_width // 2, 2), ("src", "wc", "core"))
    in_specs = (
        P("src", None, WIDTH),
        P("src", WIDTH, None),
        P("src", None),
        P("src", None, WIDTH),
        P(None, WIDTH),
        P(WIDTH),
        P(None, WIDTH),
        P(WIDTH, None),
        P(WIDTH, None),
        P(),
    )
    out_specs = (P("src", WIDTH), P("src", WIDTH))
    return jax.shard_map(
        on_device, mesh=fine, in_specs=in_specs, out_specs=out_specs, check_vma=False
    )
```

profile of v0, /device:TPU:24, one launch (start us, length us, event | category | flops | bytes accessed | tf_op | source)
XLA Modules:
  0.0 602.3 jit_solution(9003281034998828032)
XLA Ops:
  7.2 0.0 copy-start
  7.2 0.0 copy-start.4
  7.2 0.0 reduce-scatter.3.cloned.1.call-start
  7.2 1.8 copy-done
  9.1 1.3 dynamic-slice_bitcast_fusion.1
  10.3 0.0 collective-permute-start
  10.3 0.0 copy-done.4
  10.4 0.5 collective-permute-start.1
  10.9 1.0 fusion.3
  11.9 2.6 collective-permute-done.1
  14.5 0.0 collective-permute-done
  14.5 5.2 convolution_add_fusion
  19.7 0.0 reduce-scatter.3.cloned.1.call-update
  19.7 0.0 all-gather.4.cloned.1.call-start
  19.8 0.8 constant_dynamic-slice_fusion
  20.5 102.9 %reduce-scatter.3.cloned.1.call-done = f32[192,512]{1,0:T(8,128)} async-done(((f32[3072,512]{1,0:T(8,128)}), f32[192,512]{1,0:T(8,128)}) %reduce-scatter.3.cloned.1.call-update) | async-done | bytes 393232 | tf_op jit(solution)/shard_map/reduce_scatter | solution.py:43
  123.4 1.8 maximum_convert_fusion
  125.2 0.0 all-gather.4.cloned.1.call-update
  125.2 0.0 reduce-scatter.5.cloned.1.call-start
  125.3 1.5 dynamic-slice_bitcast_fusion
  126.8 0.1 collective-permute-start.2
  126.9 3.5 collective-permute-done.2
  130.4 76.5 %all-gather.4.cloned.1.call-done = bf16[3072,512]{1,0:T(8,128)(2,1)} async-done(((bf16[192,512]{1,0:T(8,128)(2,1)}), bf16[3072,512]{1,0:T(8,128)(2,1)}) %all-gather.4.cloned.1.call-update) | async-done | bytes 3145744 | tf_op jit(solution)/shard_map/all_gather | solution.py:46
  207.0 0.0 copy-start.1
  207.0 3.5 fusion.41
  210.5 0.0 copy-start.6
  210.5 0.0 copy-start.5
  210.5 0.1 collective-permute-start.3
  210.6 0.0 copy-done.1
  210.6 2.4 fusion.1
  213.1 0.0 collective-permute-done.3
  213.1 0.9 add.81
  214.0 0.0 reduce-scatter.5.cloned.1.call-update
  214.0 0.0 all-gather.6.cloned.1.call-start
  214.0 83.6 %reduce-scatter.5.cloned.1.call-done = f32[64,256]{1,0:T(8,128)} async-done(((f32[512,256]{1,0:T(8,128)}), f32[64,256]{1,0:T(8,128)}) %reduce-scatter.5.cloned.1.call-update) | async-done | bytes 65552 | tf_op jit(solution)/shard_map/reduce_scatter | solution.py:56
  297.6 1.6 convert_add_fusion
  299.2 0.0 copy-start.2
  299.2 0.0 all-gather.6.cloned.1.call-update
  299.2 0.0 copy-done.6
  299.2 0.1 dynamic_slice.46
  299.3 0.0 copy-done.5
  299.3 40.4 %all-gather = f32[32,1,256]{2,1,0:T(1,128)S(1)} all-gather(f32[1,1,256]{2,1,0:T(1,128)S(1)} %bitcast.66), channel_id=1, replica_groups=mesh['src'=8,'wc'=16,'core'=2] {'wc','core'}, dimensions={0}, use_global_device_ids=true | all-gather | bytes 33792 | tf_op jit(solution)/shard_map/all_gather | solution.py:61
  339.7 0.1 fusion.17
  339.8 15.4 %all-gather.6.cloned.1.call-done = f32[64,8192]{1,0:T(8,128)} async-done(((f32[64,256]{1,0:T(8,128)}), f32[64,8192]{1,0:T(8,128)}) %all-gather.6.cloned.1.call-update) | async-done | bytes 2097168 | tf_op jit(solution)/shard_map/all_gather | solution.py:60
  355.2 0.0 copy-start.3
  355.2 1.9 multiply_reduce_fusion
  357.1 1.3 fusion.34
  358.4 0.0 copy-done.2
  358.5 0.0 copy-done.3
  358.5 1.0 fusion.35
  359.4 140.9 %all-reduce.2 = (bf16[64,1024]{1,0:T(8,128)(2,1)}, bf16[64,1024]{1,0:T(8,128)(2,1)}) all-reduce(f32[64,1024]{1,0:T(8,128)} %fusion.35, f32[64,1024]{1,0:T(8,128)S(1)} %fusion.34), channel_id=1, replica_groups=mesh['src'=8,'wc'=16,'core'=2] {'wc','core'}, use_global_device_ids=true, to_apply=%region_3.0 | all-reduce | flops 131072 | bytes 786432 | tf_op jit(solution)/shard_map/psum | solution.py:69
  500.3 0.7 dynamic-slice_convert_fusion
  501.0 43.8 %all_gather.18 = bf16[512,128]{1,0:T(8,128)(2,1)S(1)} all-gather(bf16[64,128]{1,0:T(8,128)(2,1)S(1)} %dynamic-slice_convert_fusion), channel_id=1, replica_groups=mesh['src'=8,'wc'=16,'core'=2] {'src'}, dimensions={0}, use_global_device_ids=true | all-gather | bytes 147456 | tf_op jit(solution)/shard_map/all_gather | solution.py:74
  544.8 0.7 dynamic-slice_convert_fusion.1
  545.5 43.8 %all_gather.17 = bf16[512,128]{1,0:T(8,128)(2,1)S(1)} all-gather(bf16[64,128]{1,0:T(8,128)(2,1)S(1)} %dynamic-slice_convert_fusion.1), channel_id=1, replica_groups=mesh['src'=8,'wc'=16,'core'=2] {'src'}, dimensions={0}, use_global_device_ids=true | all-gather | bytes 147456 | tf_op jit(solution)/shard_map/all_gather | solution.py:75
  589.3 3.7 fusion.11
  593.0 1.0 fusion.36
  594.0 1.2 fusion.12
  595.2 0.6 copy.30
  (2 shorter events, 0.0 us)
Async XLA Ops:
  7.2 1.9 copy-start
  7.2 3.2 copy-start.4
  7.2 116.2 %reduce-scatter.3.cloned.1.call-start = ((), (), s32[]{:S(2)}) async-start(), calls=%async_computation.2 | async-start | bytes 6684672 | tf_op jit(solution)/shard_map/reduce_scatter | solution.py:43
  10.3 4.1 collective-permute-start
  10.4 4.1 collective-permute-start.1
  19.7 187.3 %all-gather.4.cloned.1.call-start = ((), (), s32[]{:S(2)}) async-start(), calls=%async_computation.3 | async-start | bytes 3342336 | tf_op jit(solution)/shard_map/all_gather | solution.py:46
  125.2 172.4 %reduce-scatter.5.cloned.1.call-start = ((), (), s32[]{:S(2)}) async-start(), calls=%async_computation.4 | async-start | bytes 589824 | tf_op jit(solution)/shard_map/reduce_scatter | solution.py:56
  126.8 3.6 collective-permute-start.2
  207.0 3.7 copy-start.1
  210.5 88.7 %copy-start.6 = (s32[512]{0:T(512)S(1)}, s32[512]{0:T(512)}, u32[]{:S(2)}) copy-start(s32[512]{0:T(512)} %param.19) | copy-start | bytes 6148
  210.5 88.8 %copy-start.5 = (f32[256]{0:T(256)S(1)}, f32[256]{0:T(256)}, u32[]{:S(2)}) copy-start(f32[256]{0:T(256)} %param.15) | copy-start | bytes 3076
  210.5 2.5 collective-permute-start.3
  214.0 141.2 %all-gather.6.cloned.1.call-start = ((), (), s32[]{:S(2)}) async-start(), calls=%async_computation.5 | async-start | bytes 2162688 | tf_op jit(solution)/shard_map/all_gather | solution.py:60
  299.2 59.3 %copy-start.2 = (f32[64,256]{1,0:T(8,128)S(1)}, f32[64,256]{1,0:T(8,128)}, u32[]{:S(2)}) copy-start(f32[64,256]{1,0:T(8,128)} %get-tuple-element.4) | copy-start | bytes 196612
  355.2 3.3 copy-start.3
Sparse Core Ops, SparseCore 0:
  19.8 103.5 reduce-scatter.2
  125.4 81.5 all-gather.3
  214.1 83.4 reduce-scatter.4
  299.3 55.8 all-gather.5
where the time goes:
time: 603 us; the launch traced here: 602 us
  waiting for transfers between devices  285 us (47%)
  blocking collectives  269 us (45%)
  matrix products  20.3 us (3%)
  between operations  14 us (2%)
  local copies, waits for them, and re-layouts  7.55 us (1%)
  other arithmetic  6.22 us (1%)
    psum x1, blocking collectives, on_device(): key_total, value_total = lax.psum((key_part, value_part), WIDTH)  141 us
    reduce_scatter x1, waiting for transfers between devices, on_device(): pre_share = lax.psum_scatter(pre, 'wc', scatter_dimension=0, tiled=True)  103 us
    reduce_scatter x1, waiting for transfers between devices, on_device(): mlp = lax.psum_scatter(mlp_layer, 'src', scatter_dimension=0, tiled=True)  83.6 us
    all_gather x1, waiting for transfers between devices, on_device(): feats_half = lax.all_gather(feats_t, 'wc', axis=0, tiled=True)  76.5 us
    all_gather x1, blocking collectives, on_device(): key_head = lax.all_gather(key_head, 'src', axis=0, tiled=True)  43.8 us
    all_gather x1, blocking collectives, on_device(): value_head = lax.all_gather(value_head, 'src', axis=0, tiled=True)  43.8 us
    all_gather x1, blocking collectives, on_device(): gain_full = lax.all_gather(norm_gain, WIDTH, axis=0, tiled=True)  40.4 us
    all_gather x1, waiting for transfers between devices, on_device(): stream_full = lax.all_gather(stream, WIDTH, axis=1, tiled=True)  15.4 us
  transfers between devices with their start and end apart: 8, of which 6 were waited for; matrix products, arithmetic and copies ran while one was open for 1% of the time, Pallas kernels for 0%

commit v1 on v0

--- a/solution.py
+++ b/solution.py
@@ -72,7 +72,9 @@
     key_head = lax.dynamic_slice_in_dim(key_total, kv_index * HD, HD, 1).astype(jnp.bfloat16)
     value_head = lax.dynamic_slice_in_dim(value_total, kv_index * HD, HD, 1).astype(jnp.bfloat16)
     key_head = lax.all_gather(key_head, "src", axis=0, tiled=True)
-    value_head = lax.all_gather(value_head, "src", axis=0, tiled=True)
+    value_head = jnp.concatenate(
+        lax.all_to_all(jnp.stack([value_head] * lax.axis_size("src")), "src", 0, 0), axis=0
+    )
     query3 = query.reshape(query_rows, heads_here, HD)
     scores = jnp.einsum(
         "qhd,sd->hqs", query3, key_head, preferred_element_type=jnp.float32

time: 603 us -> 573 us (0.950)
  blocking collectives: 269 us -> 225 us
  starting transfers between devices: 0.86 us -> 9.19 us
    all_gather x1 -> x0, blocking collectives: 43.8 us -> none  [on_device(): value_head = lax.all_gather(value_head, 'src', axis=0, tiled=True)]
    all_to_all x0 -> x1, starting transfers between devices: none -> 8.34 us  [on_device(): lax.all_to_all(jnp.stack([value_head] * lax.axis_size('src')), 'src', 0, 0)]
  transfers between devices with their start and end apart: 8 -> 9, of which waited for: 6 -> 7; matrix products, arithmetic and copies ran while one was open for 1% -> 2% of each run, Pallas kernels for 0% -> 0%
where the time goes in v1:
time: 573 us; the launch traced here: 571 us
  waiting for transfers between devices  288 us (50%)
  blocking collectives  225 us (39%)
  matrix products  20.3 us (4%)
  between operations  14 us (2%)
  starting transfers between devices  9.19 us (2%)
  local copies, waits for them, and re-layouts  8.22 us (1%)
  other arithmetic  6.21 us (1%)
    psum x1, blocking collectives, on_device(): key_total, value_total = lax.psum((key_part, value_part), WIDTH)  141 us
    reduce_scatter x1, waiting for transfers between devices, on_device(): pre_share = lax.psum_scatter(pre, 'wc', scatter_dimension=0, tiled=True)  103 us
    reduce_scatter x1, waiting for transfers between devices, on_device(): mlp = lax.psum_scatter(mlp_layer, 'src', scatter_dimension=0, tiled=True)  83.5 us
    all_gather x1, waiting for transfers between devices, on_device(): feats_half = lax.all_gather(feats_t, 'wc', axis=0, tiled=True)  76.5 us
    all_gather x1, blocking collectives, on_device(): key_head = lax.all_gather(key_head, 'src', axis=0, tiled=True)  43.8 us
    all_gather x1, blocking collectives, on_device(): gain_full = lax.all_gather(norm_gain, WIDTH, axis=0, tiled=True)  40.3 us
    all_gather x1, waiting for transfers between devices, on_device(): stream_full = lax.all_gather(stream, WIDTH, axis=1, tiled=True)  15.4 us
  transfers between devices with their start and end apart: 9, of which 7 were waited for; matrix products, arithmetic and copies ran while one was open for 2% of the time, Pallas kernels for 0%

profile of v1, /device:TPU:24, one launch (start us, length us, event | category | flops | bytes accessed | tf_op | source)
XLA Modules:
  0.0 571.2 jit_solution(13680922883425691608)
XLA Ops:
  7.2 0.0 copy-start
  7.2 0.0 copy-start.4
  7.2 0.0 reduce-scatter.3.cloned.1.call-start
  7.2 1.8 copy-done
  9.1 1.3 dynamic-slice_bitcast_fusion.1
  10.3 0.0 collective-permute-start
  10.4 0.0 copy-done.4
  10.4 0.5 collective-permute-start.1
  10.9 1.0 fusion.3
  11.9 2.6 collective-permute-done.1
  14.5 0.0 collective-permute-done
  14.5 5.2 convolution_add_fusion
  19.7 0.0 reduce-scatter.3.cloned.1.call-update
  19.7 0.0 all-gather.4.cloned.1.call-start
  19.8 0.8 constant_dynamic-slice_fusion
  20.5 103.0 %reduce-scatter.3.cloned.1.call-done = f32[192,512]{1,0:T(8,128)} async-done(((f32[3072,512]{1,0:T(8,128)}), f32[192,512]{1,0:T(8,128)}) %reduce-scatter.3.cloned.1.call-update) | async-done | bytes 393232 | tf_op jit(solution)/shard_map/reduce_scatter | solution.py:43
  123.5 1.8 maximum_convert_fusion
  125.3 0.0 all-gather.4.cloned.1.call-update
  125.3 0.0 reduce-scatter.5.cloned.1.call-start
  125.4 1.5 dynamic-slice_bitcast_fusion
  126.9 0.1 collective-permute-start.2
  127.0 3.5 collective-permute-done.2
  130.5 76.5 %all-gather.4.cloned.1.call-done = bf16[3072,512]{1,0:T(8,128)(2,1)} async-done(((bf16[192,512]{1,0:T(8,128)(2,1)}), bf16[3072,512]{1,0:T(8,128)(2,1)}) %all-gather.4.cloned.1.call-update) | async-done | bytes 3145744 | tf_op jit(solution)/shard_map/all_gather | solution.py:46
  207.1 0.0 copy-start.1
  207.1 3.5 fusion.40
  210.6 0.0 copy-start.6
  210.6 0.0 copy-start.5
  210.6 0.1 collective-permute-start.3
  210.7 0.0 copy-done.1
  210.7 2.4 fusion.1
  213.2 0.0 collective-permute-done.3
  213.2 0.9 add.81
  214.0 0.0 reduce-scatter.5.cloned.1.call-update
  214.1 0.0 all-gather.6.cloned.1.call-start
  214.1 83.5 %reduce-scatter.5.cloned.1.call-done = f32[64,256]{1,0:T(8,128)} async-done(((f32[512,256]{1,0:T(8,128)}), f32[64,256]{1,0:T(8,128)}) %reduce-scatter.5.cloned.1.call-update) | async-done | bytes 65552 | tf_op jit(solution)/shard_map/reduce_scatter | solution.py:56
  297.6 1.6 convert_add_fusion
  299.2 0.0 copy-start.2
  299.2 0.0 all-gather.6.cloned.1.call-update
  299.2 0.0 copy-done.6
  299.2 0.1 dynamic_slice.46
  299.3 0.0 copy-done.5
  299.3 40.3 %all-gather = f32[32,1,256]{2,1,0:T(1,128)S(1)} all-gather(f32[1,1,256]{2,1,0:T(1,128)S(1)} %bitcast.68), channel_id=1, replica_groups=mesh['src'=8,'wc'=16,'core'=2] {'wc','core'}, dimensions={0}, use_global_device_ids=true | all-gather | bytes 33792 | tf_op jit(solution)/shard_map/all_gather | solution.py:61
  339.7 0.1 fusion.16
  339.8 15.4 %all-gather.6.cloned.1.call-done = f32[64,8192]{1,0:T(8,128)} async-done(((f32[64,256]{1,0:T(8,128)}), f32[64,8192]{1,0:T(8,128)}) %all-gather.6.cloned.1.call-update) | async-done | bytes 2097168 | tf_op jit(solution)/shard_map/all_gather | solution.py:60
  355.1 0.0 copy-start.3
  355.1 1.9 multiply_reduce_fusion
  357.0 1.3 fusion.33
  358.4 0.0 copy-done.2
  358.4 0.0 copy-done.3
  358.4 0.9 fusion.34
  359.3 140.9 %all-reduce.2 = (bf16[64,1024]{1,0:T(8,128)(2,1)}, bf16[64,1024]{1,0:T(8,128)(2,1)}) all-reduce(f32[64,1024]{1,0:T(8,128)} %fusion.34, f32[64,1024]{1,0:T(8,128)S(1)} %fusion.33), channel_id=1, replica_groups=mesh['src'=8,'wc'=16,'core'=2] {'wc','core'}, use_global_device_ids=true, to_apply=%region_3.0 | all-reduce | flops 131072 | bytes 786432 | tf_op jit(solution)/shard_map/psum | solution.py:69
  500.2 0.7 dynamic-slice_convert_fusion
  501.0 43.8 %all_gather.14 = bf16[512,128]{1,0:T(8,128)(2,1)S(1)} all-gather(bf16[64,128]{1,0:T(8,128)(2,1)S(1)} %dynamic-slice_convert_fusion), channel_id=1, replica_groups=mesh['src'=8,'wc'=16,'core'=2] {'src'}, dimensions={0}, use_global_device_ids=true | all-gather | bytes 147456 | tf_op jit(solution)/shard_map/all_gather | solution.py:74
  544.7 0.7 dynamic-slice_convert_fusion.1
  545.5 0.7 stack.2
  546.1 8.3 %all-to-all-start = ((bf16[8,64,128]{2,1,0:T(8,128)(2,1)}), bf16[8,64,128]{2,1,0:T(8,128)(2,1)S(1)}, u32[]{:S(2)}, u32[]{:S(2)}) async-start(bf16[8,64,128]{2,1,0:T(8,128)(2,1)} %stack.2), calls=%async_computation.2 | async-start | bytes 262144 | tf_op jit(solution)/shard_map/all_to_all | solution.py:76
  554.5 3.7 fusion.11
  558.2 1.0 fusion.35
  559.2 3.7 all-to-all-done
  562.8 1.2 fusion.12
  564.0 0.6 copy.30
  (2 shorter events, 0.0 us)
Async XLA Ops:
  7.2 1.9 copy-start
  7.2 3.2 copy-start.4
  7.2 116.3 %reduce-scatter.3.cloned.1.call-start = ((), (), s32[]{:S(2)}) async-start(), calls=%async_computation.3 | async-start | bytes 6684672 | tf_op jit(solution)/shard_map/reduce_scatter | solution.py:43
  10.3 4.1 collective-permute-start
  10.4 4.1 collective-permute-start.1
  19.7 187.4 %all-gather.4.cloned.1.call-start = ((), (), s32[]{:S(2)}) async-start(), calls=%async_computation.4 | async-start | bytes 3342336 | tf_op jit(solution)/shard_map/all_gather | solution.py:46
  125.3 172.3 %reduce-scatter.5.cloned.1.call-start = ((), (), s32[]{:S(2)}) async-start(), calls=%async_computation.5 | async-start | bytes 589824 | tf_op jit(solution)/shard_map/reduce_scatter | solution.py:56
  126.9 3.6 collective-permute-start.2
  207.1 3.6 copy-start.1
  210.6 88.6 %copy-start.6 = (s32[512]{0:T(512)S(1)}, s32[512]{0:T(512)}, u32[]{:S(2)}) copy-start(s32[512]{0:T(512)} %param.19) | copy-start | bytes 6148
  210.6 88.7 %copy-start.5 = (f32[256]{0:T(256)S(1)}, f32[256]{0:T(256)}, u32[]{:S(2)}) copy-start(f32[256]{0:T(256)} %param.15) | copy-start | bytes 3076
  210.6 2.5 collective-permute-start.3
  214.1 141.1 %all-gather.6.cloned.1.call-start = ((), (), s32[]{:S(2)}) async-start(), calls=%async_computation.6 | async-start | bytes 2162688 | tf_op jit(solution)/shard_map/all_gather | solution.py:60
  299.2 59.2 %copy-start.2 = (f32[64,256]{1,0:T(8,128)S(1)}, f32[64,256]{1,0:T(8,128)}, u32[]{:S(2)}) copy-start(f32[64,256]{1,0:T(8,128)} %get-tuple-element.4) | copy-start | bytes 196612
  355.1 3.3 copy-start.3
  546.1 16.7 %all-to-all-start = ((bf16[8,64,128]{2,1,0:T(8,128)(2,1)}), bf16[8,64,128]{2,1,0:T(8,128)(2,1)S(1)}, u32[]{:S(2)}, u32[]{:S(2)}) async-start(bf16[8,64,128]{2,1,0:T(8,128)(2,1)} %stack.2), calls=%async_computation.2 | async-start | bytes 262144 | tf_op jit(solution)/shard_map/all_to_all | solution.py:76
Sparse Core Ops, SparseCore 0:
  19.8 103.6 reduce-scatter.2
  125.5 81.5 all-gather.3
  214.2 83.3 reduce-scatter.4
  299.3 55.7 all-gather.5
